TPU v7x, 32 devices: a whole 2x2x4 slice. The times are simulated.
32 devices in a mesh: groups: 2 (over y), ctx: 4 (over x, core), dp: 4 (over z).
Axes of the slice: x: 2, y: 2, z: 4, core: 2. Of those that a mesh axis runs over, the one named last changes fastest.
Arguments:
- hidden_in: bfloat16 [8192, 1536], P(('groups', 'ctx', 'dp')), parts along dimension 0, may hold values from -0.119628906 to 0.119628906
- queries: bfloat16 [8192, 1536], P(('groups', 'ctx', 'dp')), parts along dimension 0, may hold values from -60 to 60
- keys: bfloat16 [8192, 256], P(('groups', 'ctx', 'dp')), parts along dimension 0, may hold values from -60 to 60
- values: bfloat16 [8192, 256], P(('groups', 'ctx', 'dp')), parts along dimension 0, may hold values from -6 to 6
- out_grad: bfloat16 [8192, 1536], P(('groups', 'ctx', 'dp')), parts along dimension 0, may hold values from -48 to 48
- segment_ids: int32 [8192], P('groups'), parts along dimension 0, may hold values from 0 to 15, never falling along the last dimension, each value on 1 to 512 neighbouring positions
Outputs:
- query_grad: bfloat16 [8192, 1536], P(('groups', 'ctx', 'dp')), parts along dimension 0
- kv_weight_grad: float32 [3072, 512], P(('groups', 'dp')), parts along dimension 0
There are 2 independent parts, one for each index of `groups`. A program takes and returns all parts, laid end to end along the dimension named above; each array names one. Nothing has to cross between parts.
Inputs may be any that keep to these rules, and one draw needn't show every extreme that they name: `segment_ids`: the ids never fall along the tokens; each rollout takes 1 to 512 consecutive positions, and one takes exactly 512.
All inputs are finite; a program needn't handle non-finite values.
Results may differ from a plain program's by a relative error of at most 0.0049.
Values may be sent and summed in bfloat16 or wider, within the bound.
No kernel may reach another device: no remote copies, remote signals or barrier semaphores. Data moves between devices by JAX's collectives and lax.ppermute only.
A program may use at most 64 MiB of HBM per device.

v0:
```python
import jax
import jax.numpy as jnp
from jax import lax
from jax.sharding import PartitionSpec as P

QUERY_HEADS = 12
KEY_VALUE_HEADS = 2
HEAD_SIZE = 128


def shifted(block, axis, distance):
    devices = range(lax.axis_size(axis))
    route = [(i - distance, i) for i in devices if i - distance in devices]
    return lax.ppermute(block, axis, route)


def window_grads(block_of_query, key_span_window, value_span_window, block_gradient, visible):
    rows_per_block = block_of_query.shape[0]
    rows_in_span = key_span_window.shape[0]
    group_width = QUERY_HEADS // KEY_VALUE_HEADS
    scale = HEAD_SIZE ** (-0.5)
    heads_of_query = block_of_query.reshape(rows_per_block, KEY_VALUE_HEADS, group_width, HEAD_SIZE)
    head_gradients = block_gradient.reshape(rows_per_block, KEY_VALUE_HEADS, group_width, HEAD_SIZE)
    heads_of_key = key_span_window.reshape(rows_in_span, KEY_VALUE_HEADS, HEAD_SIZE)
    heads_of_value = value_span_window.reshape(rows_in_span, KEY_VALUE_HEADS, HEAD_SIZE)
    query_parts = []
    key_pieces = []
    value_pieces = []
    for head_position in range(KEY_VALUE_HEADS):
        query_now = heads_of_query[:, head_position]
        grad_now = head_gradients[:, head_position]
        key_now = heads_of_key[:, head_position]
        value_now = heads_of_value[:, head_position]
        scores = (
            jnp.einsum("tgd,sd->gts", query_now, key_now, preferred_element_type=jnp.float32)
            * scale
        )
        scores = jnp.where(visible[None], scores, -jnp.inf)
        top = jnp.max(scores, axis=-1, keepdims=True)
        expo = jnp.exp(scores - top)
        probs = expo / jnp.sum(expo, axis=-1, keepdims=True)
        probs_low = probs.astype(jnp.bfloat16)
        dprobs = jnp.einsum("tgd,sd->gts", grad_now, value_now, preferred_element_type=jnp.float32)
        delta = jnp.sum(probs * dprobs, axis=-1, keepdims=True)
        dscores_low = (probs * (dprobs - delta)).astype(jnp.bfloat16)
        value_pieces.append(
            jnp.einsum("gts,tgd->sd", probs_low, grad_now, preferred_element_type=jnp.float32)
        )
        key_pieces.append(
            jnp.einsum("gts,tgd->sd", dscores_low, query_now, preferred_element_type=jnp.float32)
            * scale
        )
        query_parts.append(
            jnp.einsum("gts,sd->tgd", dscores_low, key_now, preferred_element_type=jnp.float32)
            * scale
        )
    query_grad = jnp.stack(query_parts, 1).reshape(rows_per_block, QUERY_HEADS * HEAD_SIZE)
    key_gradient = jnp.stack(key_pieces, 1).reshape(rows_in_span, KEY_VALUE_HEADS * HEAD_SIZE)
    value_gradient = jnp.stack(value_pieces, 1).reshape(rows_in_span, KEY_VALUE_HEADS * HEAD_SIZE)
    return (query_grad, jnp.concatenate([key_gradient, value_gradient], 1))


def weight_term(hidden_block, kv_grad):
    return jnp.einsum(
        "td,tc->dc", hidden_block.astype(jnp.float32), kv_grad, precision=lax.Precision.HIGHEST
    )


def on_device(hidden_in, queries, keys, values, out_grad, segment_ids):
    rows_per_block = queries.shape[0]
    cycle_place = lax.axis_index(("ctx", "dp"))
    prev_keys, prev_values = shifted((keys, values), ("ctx", "dp"), 1)
    key_span_window = jnp.concatenate([prev_keys, keys], 0)
    value_span_window = jnp.concatenate([prev_values, values], 0)
    own_segments = lax.dynamic_slice_in_dim(
        segment_ids, cycle_place * rows_per_block, rows_per_block, 0
    )
    prev_segments = lax.dynamic_slice_in_dim(
        segment_ids, jnp.maximum(cycle_place - 1, 0) * rows_per_block, rows_per_block, 0
    )
    key_segments = jnp.concatenate([prev_segments, own_segments], 0)
    query_rows = jnp.arange(rows_per_block, dtype=jnp.int32)[:, None]
    key_cols = jnp.arange(2 * rows_per_block, dtype=jnp.int32)[None, :]
    visible = (key_cols <= query_rows + rows_per_block) & (
        (key_cols >= rows_per_block) | (cycle_place > 0)
    )
    visible = visible & (key_segments[None, :] == own_segments[:, None])
    query_grad, kv_window = window_grads(
        queries, key_span_window, value_span_window, out_grad, visible
    )
    returned = shifted(kv_window[:rows_per_block].astype(jnp.bfloat16), ("ctx", "dp"), -1).astype(
        jnp.float32
    )
    term = weight_term(hidden_in, kv_window[rows_per_block:] + returned)
    total_rows = term.shape[0]
    replica_count = lax.axis_size("dp")
    whole = lax.psum(term, ("ctx", "dp"))
    share = total_rows // replica_count
    weight_grad = lax.dynamic_slice_in_dim(whole, lax.axis_index("dp") * share, share, 0)
    return (query_grad.astype(jnp.bfloat16), weight_grad)


def solution(mesh):
    return jax.shard_map(
        on_device,
        mesh=mesh,
        in_specs=(
            P(("groups", "ctx", "dp"), None),
            P(("groups", "ctx", "dp"), None),
            P(("groups", "ctx", "dp"), None),
            P(("groups", "ctx", "dp"), None),
            P(("groups", "ctx", "dp"), None),
            P("groups"),
        ),
        out_specs=(P(("groups", "ctx", "dp"), None), P(("groups", "dp"), None)),
        check_vma=False,
    )
```

profile of v0, /device:TPU:0, one launch (start us, length us, event | category | flops | bytes accessed | tf_op | source)
XLA Modules:
  0.0 159.0 jit_solution(12490290141752014390)
XLA Ops:
  7.2 0.0 all-reduce.2.cloned.1.call-start
  7.2 1.1 copy.27
  8.3 4.9 %collective-permute-start.1 = (bf16[256,256]{0,1:T(8,128)(2,1)S(1)}, bf16[256,256]{0,1:T(8,128)(2,1)S(1)}, u32[]{:S(2)}, u32[]{:S(2)}) collective-permute-start(bf16[256,256]{0,1:T(8,128)(2,1)S(1)} %copy.27), channel_id=1, source_target_pairs={{0,1},{1,2},{2,3},{3,4},{4,5},{5,6},{6,7},{7,8},{8,9},{9,10},{10,1... | collective-permute-start | bytes 393224 | tf_op jit(solution)/shard_map/ppermute | solution.py:14
  13.2 1.0 copy.22
  14.3 3.5 %collective-permute-start = (bf16[256,256]{0,1:T(8,128)(2,1)S(1)}, bf16[256,256]{0,1:T(8,128)(2,1)S(1)}, u32[]{:S(2)}, u32[]{:S(2)}) collective-permute-start(bf16[256,256]{0,1:T(8,128)(2,1)S(1)} %copy.22), channel_id=1, source_target_pairs={{0,1},{1,2},{2,3},{3,4},{4,5},{5,6},{6,7},{7,8},{8,9},{9,10},{10,1... | collective-permute-start | bytes 393224 | tf_op jit(solution)/shard_map/ppermute | solution.py:14
  17.8 1.4 copy.25
  19.2 1.4 copy.30
  20.6 0.8 fusion.51
  21.5 0.2 fusion.40
  21.7 0.6 fusion.41
  22.3 0.6 fusion.43
  22.9 1.4 fusion.52
  24.3 0.6 fusion.27
  25.0 1.5 fusion.53
  26.5 0.6 fusion.2
  27.1 0.6 fusion.24
  27.8 0.6 fusion.5
  28.4 0.5 fusion.4
  28.9 0.6 fusion.31
  29.5 0.5 fusion.7
  30.0 1.1 copy-done.1
  31.1 0.6 fusion.33
  31.9 1.3 collective-permute-start.2
  33.2 9.2 %collective-permute-done.2 = bf16[256,512]{0,1:T(8,128)(2,1)S(1)} collective-permute-done((bf16[256,512]{0,1:T(8,128)(2,1)S(1)}, bf16[256,512]{0,1:T(8,128)(2,1)S(1)}, u32[]{:S(2)}, u32[]{:S(2)}) %collective-permute-start.2) | collective-permute-done | bytes 262176 | tf_op jit(solution)/shard_map/ppermute | solution.py:14
  42.4 3.1 %convolution_bitcast_fusion = f32[1536,512]{0,1:T(8,128)} fusion(bf16[256,1536]{1,0:T(8,128)(2,1)S(1)} %copy-done, f32[512,256]{0,1:T(8,128)S(1)} %bitcast.147, f32[512,256]{0,1:T(8,128)S(1)} %bitcast.145, bf16[256,512]{0,1:T(8,128)(2,1)S(1)} %collective-permute-done.2), kind=kOutput, calls=%fused_computation.2 | convolution fusion | flops 2416312320 | bytes 5242880 | tf_op jit(solution)/shard_map/td,tc->dc/dot_general | solution.py:64
  45.5 0.4 fusion.22
  45.9 1.8 %fusion.23 = bf16[256,1,6,128]{0,3,2,1:T(8,128)(2,1)S(1)} fusion(bf16[6,256,512]{1,2,0:T(8,128)(2,1)} %copy-done.1, bf16[512,2,128]{0,2,1:T(8,128)(2,1)S(1)} %bitcast.156), kind=kOutput, calls=%fused_computation.36 | convolution fusion | flops 201719808 | bytes 2097152 | tf_op jit(solution)/shard_map/gts,sd->tgd/dot_general | solution.py:54
  47.7 0.1 pad_maximum_fusion
  47.8 1.2 copy.48
  48.9 100.9 %all-reduce.2.cloned.1.call-done = f32[1536,512]{0,1:T(8,128)} async-done(((f32[1536,512]{0,1:T(8,128)}), f32[1536,512]{0,1:T(8,128)}) %all-reduce.2.cloned.1.call-update) | async-done | bytes 3145744 | tf_op jit(solution)/shard_map/psum | solution.py:97
  149.9 1.2 constant_dynamic-slice_fusion
  151.0 1.1 copy.49
  (14 shorter events, 0.2 us)
Async XLA Ops:
  7.2 35.2 %copy-start = (bf16[256,1536]{1,0:T(8,128)(2,1)S(1)}, bf16[256,1536]{1,0:T(8,128)(2,1)}, u32[]{:S(2)}) copy-start(bf16[256,1536]{1,0:T(8,128)(2,1)} %param.6) | copy-start | bytes 2359300
  7.2 142.7 %all-reduce.2.cloned.1.call-start = ((), (), s32[]{:S(2)}) async-start(), calls=%async_computation | async-start | bytes 6291456 | tf_op jit(solution)/shard_map/psum | solution.py:97
  8.3 18.2 %collective-permute-start.1 = (bf16[256,256]{0,1:T(8,128)(2,1)S(1)}, bf16[256,256]{0,1:T(8,128)(2,1)S(1)}, u32[]{:S(2)}, u32[]{:S(2)}) collective-permute-start(bf16[256,256]{0,1:T(8,128)(2,1)S(1)} %copy.27), channel_id=1, source_target_pairs={{0,1},{1,2},{2,3},{3,4},{4,5},{5,6},{6,7},{7,8},{8,9},{9,10},{10,1... | collective-permute-start | bytes 393224 | tf_op jit(solution)/shard_map/ppermute | solution.py:14
  14.3 7.4 %collective-permute-start = (bf16[256,256]{0,1:T(8,128)(2,1)S(1)}, bf16[256,256]{0,1:T(8,128)(2,1)S(1)}, u32[]{:S(2)}, u32[]{:S(2)}) collective-permute-start(bf16[256,256]{0,1:T(8,128)(2,1)S(1)} %copy.22), channel_id=1, source_target_pairs={{0,1},{1,2},{2,3},{3,4},{4,5},{5,6},{6,7},{7,8},{8,9},{9,10},{10,1... | collective-permute-start | bytes 393224 | tf_op jit(solution)/shard_map/ppermute | solution.py:14
  30.0 1.1 copy-start.1
  31.9 10.5 %collective-permute-start.2 = (bf16[256,512]{0,1:T(8,128)(2,1)S(1)}, bf16[256,512]{0,1:T(8,128)(2,1)S(1)}, u32[]{:S(2)}, u32[]{:S(2)}) collective-permute-start(bf16[256,512]{0,1:T(8,128)(2,1)S(1)} %fusion.37), channel_id=1, source_target_pairs={{1,0},{2,1},{3,2},{4,3},{5,4},{6,5},{7,6},{8,7},{9,8},{10,9},{11,1... | collective-permute-start | bytes 786440 | tf_op jit(solution)/shard_map/ppermute | solution.py:14
Sparse Core Ops, SparseCore 0:
  45.6 104.1 all-reduce.1
where the time goes:
time: 159 us
  waiting for transfers between devices  110 us (69%)
  between operations  14.3 us (9%)
  local copies, waits for them, and re-layouts  10.4 us (7%)
  matrix products  10.2 us (6%)
  starting transfers between devices  9.75 us (6%)
  other arithmetic  4.31 us (3%)
    psum x1, waiting for transfers between devices, on_device(): whole = lax.psum(term, ('ctx', 'dp'))  101 us
    ppermute x3, starting transfers between devices, shifted(): return lax.ppermute(block, axis, route)  9.71 us
    ppermute x3, waiting for transfers between devices, shifted(): return lax.ppermute(block, axis, route)  9.19 us
    unnamed x10, local copies, waits for them, and re-layouts  8.33 us
  transfers between devices with their start and end apart: 4, of which 2 were waited for; matrix products, arithmetic and copies ran while one was open for 8% of the time, Pallas kernels for 0%

commit v1 on v0

--- a/solution.py
+++ b/solution.py
@@ -94,7 +94,7 @@
     term = weight_term(hidden_in, kv_window[rows_per_block:] + returned)
     total_rows = term.shape[0]
     replica_count = lax.axis_size("dp")
-    whole = lax.psum(term, ("ctx", "dp"))
+    whole = lax.psum(lax.psum(term, "dp"), "ctx")
     share = total_rows // replica_count
     weight_grad = lax.dynamic_slice_in_dim(whole, lax.axis_index("dp") * share, share, 0)
     return (query_grad.astype(jnp.bfloat16), weight_grad)

time: 159 us -> 247 us (1.55)
  waiting for transfers between devices: 110 us -> 197 us
    psum x1 -> x2, waiting for transfers between devices: 101 us -> 188 us  [on_device(): whole = lax.psum(lax.psum(term, 'dp'), 'ctx')]
  transfers between devices with their start and end apart: 4 -> 5, of which waited for: 2 -> 3; matrix products, arithmetic and copies ran while one was open for 8% -> 5% of each run, Pallas kernels for 0% -> 0%
where the time goes in v1:
time: 247 us; the launch traced here: 246 us
  waiting for transfers between devices  197 us (80%)
  between operations  14.3 us (6%)
  local copies, waits for them, and re-layouts  10.4 us (4%)
  matrix products  10.2 us (4%)
  starting transfers between devices  9.79 us (4%)
  other arithmetic  4.31 us (2%)
    psum x2, waiting for transfers between devices, on_device(): whole = lax.psum(lax.psum(term, 'dp'), 'ctx')  188 us
    ppermute x3, starting transfers between devices, shifted(): return lax.ppermute(block, axis, route)  9.71 us
    ppermute x3, waiting for transfers between devices, shifted(): return lax.ppermute(block, axis, route)  9.19 us
    unnamed x10, local copies, waits for them, and re-layouts  8.33 us
  transfers between devices with their start and end apart: 5, of which 3 were waited for; matrix products, arithmetic and copies ran while one was open for 5% of the time, Pallas kernels for 0%

profile of v1, /device:TPU:0, one launch (start us, length us, event | category | flops | bytes accessed | tf_op | source)
XLA Modules:
  0.0 246.5 jit_solution(12825689539214373772)
XLA Ops:
  7.2 1.1 copy.27
  8.3 4.9 %collective-permute-start.1 = (bf16[256,256]{0,1:T(8,128)(2,1)S(1)}, bf16[256,256]{0,1:T(8,128)(2,1)S(1)}, u32[]{:S(2)}, u32[]{:S(2)}) collective-permute-start(bf16[256,256]{0,1:T(8,128)(2,1)S(1)} %copy.27), channel_id=1, source_target_pairs={{0,1},{1,2},{2,3},{3,4},{4,5},{5,6},{6,7},{7,8},{8,9},{9,10},{10,1... | collective-permute-start | bytes 393224 | tf_op jit(solution)/shard_map/ppermute | solution.py:14
  13.2 1.0 copy.22
  14.3 3.5 %collective-permute-start = (bf16[256,256]{0,1:T(8,128)(2,1)S(1)}, bf16[256,256]{0,1:T(8,128)(2,1)S(1)}, u32[]{:S(2)}, u32[]{:S(2)}) collective-permute-start(bf16[256,256]{0,1:T(8,128)(2,1)S(1)} %copy.22), channel_id=1, source_target_pairs={{0,1},{1,2},{2,3},{3,4},{4,5},{5,6},{6,7},{7,8},{8,9},{9,10},{10,1... | collective-permute-start | bytes 393224 | tf_op jit(solution)/shard_map/ppermute | solution.py:14
  17.8 1.4 copy.25
  19.2 1.4 copy.30
  20.6 0.8 fusion.51
  21.5 0.2 fusion.40
  21.7 0.6 fusion.41
  22.3 0.6 fusion.43
  22.9 1.4 fusion.52
  24.3 0.7 fusion.27
  25.0 1.5 fusion.53
  26.5 0.6 fusion.2
  27.1 0.6 fusion.24
  27.8 0.6 fusion.5
  28.4 0.5 fusion.4
  28.9 0.6 fusion.31
  29.5 0.5 fusion.7
  30.0 1.1 copy-done.1
  31.1 0.6 fusion.33
  31.9 1.3 collective-permute-start.2
  33.2 9.2 %collective-permute-done.2 = bf16[256,512]{0,1:T(8,128)(2,1)S(1)} collective-permute-done((bf16[256,512]{0,1:T(8,128)(2,1)S(1)}, bf16[256,512]{0,1:T(8,128)(2,1)S(1)}, u32[]{:S(2)}, u32[]{:S(2)}) %collective-permute-start.2) | collective-permute-done | bytes 262176 | tf_op jit(solution)/shard_map/ppermute | solution.py:14
  42.4 3.1 %convolution_bitcast_fusion = f32[1536,512]{0,1:T(8,128)} fusion(bf16[256,1536]{1,0:T(8,128)(2,1)S(1)} %copy-done, f32[512,256]{0,1:T(8,128)S(1)} %bitcast.147, f32[512,256]{0,1:T(8,128)S(1)} %bitcast.145, bf16[256,512]{0,1:T(8,128)(2,1)S(1)} %collective-permute-done.2), kind=kOutput, calls=%fused_computation.2 | convolution fusion | flops 2416312320 | bytes 5242880 | tf_op jit(solution)/shard_map/td,tc->dc/dot_general | solution.py:64
  45.6 121.9 %all-reduce.3.cloned.1.call-done = f32[1536,512]{0,1:T(8,128)} async-done(((f32[1536,512]{0,1:T(8,128)}), f32[1536,512]{0,1:T(8,128)}) %all-reduce.3.cloned.1.call-update) | async-done | bytes 3145744 | tf_op jit(solution)/shard_map/psum | solution.py:97
  167.4 0.4 fusion.22
  167.8 1.8 fusion.23
  169.6 0.1 pad_maximum_fusion
  169.7 1.2 copy.48
  170.9 66.4 %all-reduce.5.cloned.1.call-done = f32[1536,512]{0,1:T(8,128)} async-done(((f32[1536,512]{0,1:T(8,128)}), f32[1536,512]{0,1:T(8,128)}) %all-reduce.5.cloned.1.call-update) | async-done | bytes 3145744 | tf_op jit(solution)/shard_map/psum | solution.py:97
  237.3 1.2 constant_dynamic-slice_fusion
  238.5 1.1 copy.49
  (17 shorter events, 0.3 us)
Async XLA Ops:
  7.2 35.2 %copy-start = (bf16[256,1536]{1,0:T(8,128)(2,1)S(1)}, bf16[256,1536]{1,0:T(8,128)(2,1)}, u32[]{:S(2)}) copy-start(bf16[256,1536]{1,0:T(8,128)(2,1)} %param.6) | copy-start | bytes 2359300
  7.2 160.2 %all-reduce.3.cloned.1.call-start = ((), (), s32[]{:S(2)}) async-start(), calls=%async_computation | async-start | bytes 6291456 | tf_op jit(solution)/shard_map/psum | solution.py:97
  8.3 18.2 %collective-permute-start.1 = (bf16[256,256]{0,1:T(8,128)(2,1)S(1)}, bf16[256,256]{0,1:T(8,128)(2,1)S(1)}, u32[]{:S(2)}, u32[]{:S(2)}) collective-permute-start(bf16[256,256]{0,1:T(8,128)(2,1)S(1)} %copy.27), channel_id=1, source_target_pairs={{0,1},{1,2},{2,3},{3,4},{4,5},{5,6},{6,7},{7,8},{8,9},{9,10},{10,1... | collective-permute-start | bytes 393224 | tf_op jit(solution)/shard_map/ppermute | solution.py:14
  14.3 7.4 %collective-permute-start = (bf16[256,256]{0,1:T(8,128)(2,1)S(1)}, bf16[256,256]{0,1:T(8,128)(2,1)S(1)}, u32[]{:S(2)}, u32[]{:S(2)}) collective-permute-start(bf16[256,256]{0,1:T(8,128)(2,1)S(1)} %copy.22), channel_id=1, source_target_pairs={{0,1},{1,2},{2,3},{3,4},{4,5},{5,6},{6,7},{7,8},{8,9},{9,10},{10,1... | collective-permute-start | bytes 393224 | tf_op jit(solution)/shard_map/ppermute | solution.py:14
  30.0 1.1 copy-start.1
  31.9 10.5 %collective-permute-start.2 = (bf16[256,512]{0,1:T(8,128)(2,1)S(1)}, bf16[256,512]{0,1:T(8,128)(2,1)S(1)}, u32[]{:S(2)}, u32[]{:S(2)}) collective-permute-start(bf16[256,512]{0,1:T(8,128)(2,1)S(1)} %fusion.37), channel_id=1, source_target_pairs={{1,0},{2,1},{3,2},{4,3},{5,4},{6,5},{7,6},{8,7},{9,8},{10,9},{11,1... | collective-permute-start | bytes 786440 | tf_op jit(solution)/shard_map/ppermute | solution.py:14
  45.5 191.8 %all-reduce.5.cloned.1.call-start = ((), (), s32[]{:S(2)}) async-start(), calls=%async_computation.1 | async-start | bytes 6291456 | tf_op jit(solution)/shard_map/psum | solution.py:97
Sparse Core Ops, SparseCore 0:
  45.6 121.7 all-reduce.2
  169.8 67.4 all-reduce.4
